TPU v7x, 128 devices: a whole 4x4x4 slice. The times are simulated.
128 devices in a mesh: pipe: 4 (over x_hi, core), dp: 16 (over y, z), tensor: 2 (over x_lo).
Axes of the slice: x: 4 (x_hi: 2, x_lo: 2; x = x_hi * 2 + x_lo), y: 4, z: 4, core: 2. Of those that a mesh axis runs over, the one named last changes fastest.
Arguments:
- hidden_states: bfloat16 [4, 4096, 8192], P('pipe', 'dp'), may hold values from -60 to 60
- norm_gain: bfloat16 [4, 8192], P('pipe'), may hold values from 0.5 to 2
- key_weight: bfloat16 [4, 8192, 512], P('pipe', 'dp', 'tensor'), may hold values from -0.0625 to 0.0625
- value_weight: bfloat16 [4, 8192, 512], P('pipe', 'dp', 'tensor'), may hold values from -0.0625 to 0.0625
- queries: bfloat16 [4, 4096, 4096], P('pipe', 'dp', 'tensor'), may hold values from -128 to 128
- context_cotangent: bfloat16 [4, 4096, 4096], P('pipe', 'dp', 'tensor'), may hold values from -96 to 96
- lengths: int32 [4, 16], P('pipe', 'dp'), may hold values from 64 to 256, as said below
- policy_logp: float32 [4, 16], P('pipe', 'dp'), may hold values from -90 to -30
- reference_logp: float32 [4, 16], P('pipe', 'dp'), may hold values from -90 to -30
Outputs:
- key_weight_grad: bfloat16 [4, 8192, 512], P('pipe', 'dp', 'tensor')
- value_weight_grad: bfloat16 [4, 8192, 512], P('pipe', 'dp', 'tensor')
- lower_cotangent: bfloat16 [4, 4096, 8192], P('pipe', 'dp')
Inputs may be any that keep to these rules, and one draw needn't show every extreme that they name: `lengths`: each sequence's live tokens; positions at or beyond it are padding.
All inputs are finite; a program needn't handle non-finite values.
Results may differ from a plain program's by a relative error of at most 0.015.
The roundings to bfloat16 on the way count: a program that leaves them out, or rounds other values in their place, can miss the bound.
Values may be sent and summed in bfloat16 or wider, within the bound.
No kernel may reach another device: no remote copies, remote signals or barrier semaphores. Data moves between devices by JAX's collectives and lax.ppermute only.
A program may use at most 128 MiB of HBM per device.

v0:
```python
import math
import jax
import jax.numpy as jnp
from jax import lax
from jax.sharding import PartitionSpec as P

HD = 128
npo_beta = 0.1
norm_eps = 1e-05
rope_base = 500000.0


def shifted(value, axis, steps):
    count = lax.axis_size(axis)
    leading, last = (max(0, -steps), min(count, count - steps))
    return lax.ppermute(value, axis, [(source, source + steps) for source in range(leading, last)])


def rope_tables(length, head_dim):
    positions = jnp.arange(length).astype(jnp.float32)
    freq_index = jnp.arange(head_dim // 2).astype(jnp.float32)
    inverse = 1.0 / rope_base ** (2.0 * freq_index / head_dim)
    angles = positions[:, None] * inverse[None, :]
    cosine = jnp.concatenate([jnp.cos(angles), jnp.cos(angles)], axis=1)
    sine = jnp.concatenate([jnp.sin(angles), jnp.sin(angles)], axis=1)
    return (cosine, sine)


def rotate_half(values):
    half = values.shape[-1] // 2
    return jnp.concatenate([-values[..., half:], values[..., :half]], axis=-1)


def rotate_back(values):
    half = values.shape[-1] // 2
    return jnp.concatenate([values[..., half:], -values[..., :half]], axis=-1)


def sequence_grads(query_seq, key_seq, value_seq, cotan_seq, length_seq, cosine, sine):
    seq_len, kv_heads, head_dim = key_seq.shape
    group = query_seq.shape[1] // kv_heads
    scale = 1.0 / math.sqrt(head_dim)
    query_g = query_seq.reshape(seq_len, kv_heads, group, head_dim)
    cotan_g = cotan_seq.reshape(seq_len, kv_heads, group, head_dim)
    scores = (
        jnp.einsum("ikgd,jkd->kgij", query_g, key_seq, preferred_element_type=jnp.float32) * scale
    )
    row_pos = jnp.arange(seq_len)[:, None]
    col_pos = jnp.arange(seq_len)[None, :]
    allowed = (col_pos <= row_pos) & (col_pos < length_seq)
    scores = jnp.where(allowed, scores, -1e30)
    highest = jnp.max(scores, axis=-1, keepdims=True)
    expd = jnp.where(allowed, jnp.exp(scores - highest), 0.0)
    probs = expd / jnp.sum(expd, axis=-1, keepdims=True)
    probs_low = probs.astype(jnp.bfloat16)
    value_grad = jnp.einsum(
        "kgij,ikgd->jkd", probs_low, cotan_g, preferred_element_type=jnp.float32
    ).astype(jnp.bfloat16)
    prob_grad = jnp.einsum("ikgd,jkd->kgij", cotan_g, value_seq, preferred_element_type=jnp.float32)
    centre = jnp.sum(probs * prob_grad, axis=-1, keepdims=True)
    score_grad = (probs * (prob_grad - centre) * scale).astype(jnp.bfloat16)
    rotated_grad = jnp.einsum(
        "kgij,ikgd->jkd", score_grad, query_g, preferred_element_type=jnp.float32
    )
    key_grad = rotated_grad * cosine[:, None, :] + rotate_back(rotated_grad * sine[:, None, :])
    return (key_grad.astype(jnp.bfloat16), value_grad)


def norm_backward(normed_grad, gain_f, nhat, inv_rms):
    gain_grad_in = normed_grad * gain_f
    centre = jnp.mean(gain_grad_in * nhat, axis=-1, keepdims=True)
    return ((gain_grad_in - nhat * centre) * inv_rms).astype(jnp.bfloat16)


def on_device(
    hidden_states,
    norm_gain,
    key_weight,
    value_weight,
    queries,
    context_cotangent,
    lengths,
    policy_logp,
    reference_logp,
):
    key_full, value_full = (
        lax.all_gather(key_weight[0], "dp", axis=0, tiled=True),
        lax.all_gather(value_weight[0], "dp", axis=0, tiled=True),
    )
    hidden = hidden_states[0]
    gain_f = norm_gain[0].astype(jnp.float32)
    tok_rows = hidden.shape[0]
    seq_count = lengths.shape[1]
    seq_len = tok_rows // seq_count
    kv_cols = key_full.shape[1]
    kv_local = kv_cols // HD
    q_local = queries.shape[2] // HD
    hidden_f = hidden.astype(jnp.float32)
    inv_rms = lax.rsqrt(jnp.mean(hidden_f * hidden_f, axis=-1, keepdims=True) + norm_eps)
    nhat = hidden_f * inv_rms
    normed = (nhat * gain_f).astype(jnp.bfloat16)
    key_raw = jnp.dot(normed, key_full, preferred_element_type=jnp.float32)
    values = jnp.dot(normed, value_full, preferred_element_type=jnp.float32).astype(jnp.bfloat16)
    cosine, sine = rope_tables(seq_len, HD)
    key_four = key_raw.reshape(seq_count, seq_len, kv_local, HD)
    keys = (
        key_four * cosine[None, :, None, :] + rotate_half(key_four) * sine[None, :, None, :]
    ).astype(jnp.bfloat16)
    total_seqs = seq_count * lax.axis_size("dp")
    seq_weight = 2.0 * jax.nn.sigmoid(npo_beta * (policy_logp[0] - reference_logp[0])) / total_seqs
    live = jnp.arange(seq_len)[None, :] < lengths[0][:, None]
    factor = jnp.where(live, seq_weight[:, None], 0.0)
    scaled = (
        context_cotangent[0].reshape(seq_count, seq_len, q_local, HD).astype(jnp.float32)
        * factor[:, :, None, None]
    ).astype(jnp.bfloat16)

    def one_sequence(items):
        return sequence_grads(items[0], items[1], items[2], items[3], items[4], cosine, sine)

    key_grad, value_grad = lax.map(
        one_sequence,
        (
            queries[0].reshape(seq_count, seq_len, q_local, HD),
            keys,
            values.reshape(seq_count, seq_len, kv_local, HD),
            scaled,
            lengths[0],
        ),
    )
    key_grad = key_grad.reshape(tok_rows, kv_cols)
    value_grad = value_grad.reshape(tok_rows, kv_cols)
    combined = jnp.concatenate([key_grad, value_grad], axis=1)
    grad_total = lax.psum_scatter(
        lax.dot_general(
            normed, combined, (((0,), (0,)), ((), ())), preferred_element_type=jnp.float32
        ).astype(jnp.bfloat16),
        "dp",
        scatter_dimension=0,
        tiled=True,
    )
    part = lax.dot_general(
        key_grad, key_full, (((1,), (1,)), ((), ())), preferred_element_type=jnp.float32
    )
    part = part + lax.dot_general(
        value_grad, value_full, (((1,), (1,)), ((), ())), preferred_element_type=jnp.float32
    )
    normed_grad = lax.psum(part.astype(jnp.bfloat16), "tensor").astype(jnp.float32)
    section_cot = norm_backward(normed_grad, gain_f, nhat, inv_rms)
    lower = shifted(section_cot, "pipe", -1)
    return (grad_total[:, :kv_cols][None], grad_total[:, kv_cols:][None], lower[None])


def solution(mesh):
    in_specs = (
        P("pipe", "dp", None),
        P("pipe", None),
        P("pipe", "dp", "tensor"),
        P("pipe", "dp", "tensor"),
        P("pipe", "dp", "tensor"),
        P("pipe", "dp", "tensor"),
        P("pipe", "dp"),
        P("pipe", "dp"),
        P("pipe", "dp"),
    )
    out_specs = (P("pipe", "dp", "tensor"), P("pipe", "dp", "tensor"), P("pipe", "dp", None))
    return jax.shard_map(
        on_device, mesh=mesh, in_specs=in_specs, out_specs=out_specs, check_vma=False
    )
```

profile of v0, /device:TPU:0, one launch (start us, length us, event | category | flops | bytes accessed | tf_op | source)
XLA Modules:
  0.0 366.4 jit_solution(2905376184291214419)
XLA Ops:
  7.2 0.0 copy-start.3
  7.2 0.0 all-gather.5.cloned.1.call-start
  7.2 0.7 all-gather.5.cloned.1.call-update
  7.9 0.0 all-gather.7.cloned.1.call-start
  8.0 0.7 all-gather.7.cloned.1.call-update
  8.7 0.0 all-reduce.2.cloned.1.call-start
  10.7 0.8 mul.201
  11.5 0.3 multiply_cosine_fusion
  11.9 0.8 copy.12
  12.6 0.8 copy.16
  13.4 2.3 copy.36
  15.7 0.0 copy-done.3
  15.7 0.5 copy.33
  16.2 3.1 fusion.11
  19.3 0.1 fusion.49
  19.4 44.9 %all-gather.5.cloned.1.call-done = bf16[1,8192,256]{2,1,0:T(8,128)(2,1)} async-done(((bf16[1,512,256]{2,1,0:T(8,128)(2,1)}), bf16[1,8192,256]{2,1,0:T(8,128)(2,1)}) %all-gather.5.cloned.1.call-update) | async-done | bytes 4194320 | tf_op jit(solution)/shard_map/all_gather | solution.py:87
  64.3 5.5 %fusion.20 = f32[256,256]{0,1:T(8,128)S(1)} fusion(bf16[1,8192,256]{2,1,0:T(8,128)(2,1)} %all-gather.5.cloned.1.call-done, bf16[1,256,8192]{2,1,0:T(8,128)(2,1)} %param.9, f32[8192]{0:T(1024)S(1)} %bitcast.110, f32[256]{0:T(256)S(1)} %add_rsqrt_fusion), kind=kOutput, calls=%fused_computation.28 | convolution fusion | flops 1082130432 | bytes 8684544 | tf_op jit(solution)/shard_map/dot_general | solution.py:102
  69.9 0.8 copy.13
  70.7 0.1 copy.34
  70.9 0.8 copy.35
  71.7 0.7 negate_bitcast_fusion
  72.4 45.3 %all-gather.7.cloned.1.call-done = bf16[1,8192,256]{2,1,0:T(8,128)(2,1)} async-done(((bf16[1,512,256]{2,1,0:T(8,128)(2,1)}), bf16[1,8192,256]{2,1,0:T(8,128)(2,1)}) %all-gather.7.cloned.1.call-update) | async-done | bytes 4194320 | tf_op jit(solution)/shard_map/all_gather | solution.py:88
  117.7 5.6 %fusion.37 = bf16[256,256]{0,1:T(8,128)(2,1)S(1)} fusion(bf16[1,8192,256]{2,1,0:T(8,128)(2,1)} %all-gather.7.cloned.1.call-done, bf16[1,256,8192]{2,1,0:T(8,128)(2,1)} %param.9, f32[8192]{0:T(1024)S(1)} %bitcast.111, f32[256]{0:T(256)S(1)} %add_rsqrt_fusion), kind=kOutput, calls=%fused_computation.44 | convolution fusion | flops 1082195968 | bytes 8553472 | tf_op jit(solution)/shard_map/dot_general | solution.py:103
  123.3 0.0 copy-start.4
  123.3 2.7 fusion.40
  126.0 0.0 copy-done.4
  126.0 5.0 %fusion.61 = (f32[2,8,256]{2,1,0:T(8,128)S(1)}, f32[2,8,256,256]{2,3,1,0:T(8,128)}) fusion(pred[256,256]{0,1:T(8,128)(4,1)S(1)} %fusion.49, bf16[256,2,8,128]{0,3,2,1:T(8,128)(2,1)S(1)} %bitcast.104, f32[256,2,64]{2,0,1:T(8,128)} %bitcast.115, f32[256,2,64]{2,0,1:T(8,128)} %negate_bitcast_fusion, f32[256,2,128]{2,0,1:T(8,128)} %copy.13, ...), kind=kOutput, calls=%fused_computation.80 | convolution fusion | flops 274006272 | bytes 6111232 | tf_op jit(solution)/shard_map/while/body/eval_jaxpr/sub | solution.py:53
  131.1 3.7 %fusion.34 = bf16[2,128,256]{2,1,0:T(8,128)(2,1)} fusion(f32[256,2,8,128]{0,3,2,1:T(8,128)S(1)} %bitcast.103, f32[256]{0:T(256)S(1)} %broadcast_select_fusion, f32[2,8,256,256]{2,3,1,0:T(8,128)} %get-tuple-element.42, f32[2,8,256]{2,1,0:T(8,128)S(1)} %get-tuple-element.41), kind=kOutput, calls=%fused_computation.43 | convolution fusion | flops 271646720 | bytes 6439936 | tf_op jit(solution)/shard_map/while/body/eval_jaxpr/kgij,ikgd->jkd/dot_general | solution.py:56
  134.7 7.2 %fusion.30 = f32[2,256,128]{1,2,0:T(8,128)S(1)} fusion(bf16[256,2,8,128]{0,3,2,1:T(8,128)(2,1)S(1)} %bitcast.105, f32[2,256,256,8]{2,1,3,0:T(8,128)} %fusion.40, f32[2,8,256,256]{2,3,1,0:T(8,128)} %get-tuple-element.42, f32[2,8,256]{2,1,0:T(8,128)S(1)} %get-tuple-element.41), kind=kOutput, calls=%fused_computation.41 | convolution fusion | flops 275779840 | bytes 9715712 | tf_op jit(solution)/shard_map/while/body/eval_jaxpr/kgij,ikgd->jkd/dot_general | solution.py:62
  142.1 0.0 copy-start.2
  142.1 0.0 copy-start.5
  142.1 3.6 fusion.18
  145.8 0.0 copy-done.2
  145.8 0.0 copy-done.5
  145.8 3.6 fusion.5
  149.4 0.0 all-reduce.2.cloned.1.call-update
  149.5 0.0 reduce-scatter.2.cloned.1.call-start
  149.5 7.9 %convolution_convert_fusion = bf16[8192,512]{1,0:T(8,128)(2,1)} fusion(bf16[256,256]{0,1:T(8,128)(2,1)S(1)} %bitcast.117, bf16[256,256]{0,1:T(8,128)(2,1)S(1)} %bitcast.109, bf16[1,256,8192]{2,1,0:T(8,128)(2,1)} %param.9, f32[8192]{0:T(1024)S(1)} %bitcast.112, f32[256]{0:T(256)S(1)} %add_rsqrt_fusion), kind=kOutput, calls=%fused_computation.2 | convolution fusion | flops 2160590848 | bytes 12878848 | tf_op jit(solution)/shard_map/dot_general | solution.py:135
  157.4 0.0 reduce-scatter.2.cloned.1.call-update
  157.5 106.2 %all-reduce.2.cloned.1.call-done = bf16[256,8192]{1,0:T(8,128)(2,1)} async-done(((bf16[256,8192]{1,0:T(8,128)(2,1)}), bf16[256,8192]{1,0:T(8,128)(2,1)}) %all-reduce.2.cloned.1.call-update) | async-done | bytes 4194320 | tf_op jit(solution)/shard_map/psum | solution.py:148
  263.6 0.0 copy-start
  263.6 0.0 copy-start.1
  263.6 5.4 %fusion.7 = f32[256]{0:T(256)S(1)} fusion(bf16[256,8192]{1,0:T(8,128)(2,1)} %all-reduce.2.cloned.1.call-done, bf16[1,256,8192]{2,1,0:T(8,128)(2,1)} %param.9, f32[8192]{0:T(1024)S(1)} %bitcast.113, f32[256]{0:T(256)S(1)} %add_rsqrt_fusion), kind=kLoop, calls=%fused_computation.11 | loop fusion | flops 12582656 | bytes 8423424 | tf_op jit(solution)/shard_map/reduce_sum | solution.py:71
  269.0 0.0 copy-done
  269.0 0.5 copy-done.1
  269.6 2.3 fusion.10
  271.8 1.3 collective-permute-start
  273.1 7.9 %collective-permute-done = bf16[256,8192]{1,0:T(8,128)(2,1)} collective-permute-done((bf16[256,8192]{1,0:T(8,128)(2,1)S(1)}, bf16[256,8192]{1,0:T(8,128)(2,1)}, u32[]{:S(2)}, u32[]{:S(2)}) %collective-permute-start) | collective-permute-done | bytes 4194336 | tf_op jit(solution)/shard_map/ppermute | solution.py:16
  281.0 72.4 %reduce-scatter.2.cloned.1.call-done = bf16[512,512]{1,0:T(8,128)(2,1)} async-done(((bf16[8192,512]{1,0:T(8,128)(2,1)}), bf16[512,512]{1,0:T(8,128)(2,1)}) %reduce-scatter.2.cloned.1.call-update) | async-done | bytes 524304 | tf_op jit(solution)/shard_map/reduce_scatter | solution.py:134
  353.4 1.9 slice_bitcast_fusion
  355.3 4.6 %copy.42 = bf16[1,256,8192]{2,1,0:T(8,128)(2,1)} copy(bf16[1,256,8192]{2,1,0:T(8,128)(2,1)} %bitcast.30) | data formatting | bytes 8388608
  (11 shorter events, 0.2 us)
Async XLA Ops:
  7.2 8.5 %copy-start.3 = (bf16[1,256,2048]{2,1,0:T(8,128)(2,1)S(1)}, bf16[1,256,2048]{2,1,0:T(8,128)(2,1)}, u32[]{:S(2)}) copy-start(bf16[1,256,2048]{2,1,0:T(8,128)(2,1)} %param.14) | copy-start | bytes 3145732
  7.2 57.1 %all-gather.5.cloned.1.call-start = ((), (), s32[]{:S(2)}) async-start(), calls=%async_computation.3 | async-start | bytes 4456448 | tf_op jit(solution)/shard_map/all_gather | solution.py:87
  7.9 109.8 %all-gather.7.cloned.1.call-start = ((), (), s32[]{:S(2)}) async-start(), calls=%async_computation.4 | async-start | bytes 4456448 | tf_op jit(solution)/shard_map/all_gather | solution.py:88
  8.7 255.0 %all-reduce.2.cloned.1.call-start = ((), (), s32[]{:S(2)}) async-start(), calls=%async_computation.2 | async-start | bytes 8388608 | tf_op jit(solution)/shard_map/psum | solution.py:148
  123.3 2.7 copy-start.4
  142.1 3.7 %copy-start.2 = (bf16[1,8192,256]{2,1,0:T(8,128)(2,1)S(1)}, bf16[1,8192,256]{2,1,0:T(8,128)(2,1)}, u32[]{:S(2)}) copy-start(bf16[1,8192,256]{2,1,0:T(8,128)(2,1)} %all-gather.7.cloned.1.call-done) | copy-start | bytes 12582916
  142.1 3.7 %copy-start.5 = (bf16[2,128,256]{2,1,0:T(8,128)(2,1)S(1)}, bf16[2,128,256]{2,1,0:T(8,128)(2,1)}, u32[]{:S(2)}) copy-start(bf16[2,128,256]{2,1,0:T(8,128)(2,1)} %fusion.34) | copy-start | bytes 393220
  149.5 204.0 %reduce-scatter.2.cloned.1.call-start = ((), (), s32[]{:S(2)}) async-start(), calls=%async_computation.1 | async-start | bytes 8912896 | tf_op jit(solution)/shard_map/reduce_scatter | solution.py:134
  263.6 5.4 %copy-start = (bf16[1,256,8192]{2,1,0:T(8,128)(2,1)S(1)}, bf16[1,256,8192]{2,1,0:T(8,128)(2,1)}, u32[]{:S(2)}) copy-start(bf16[1,256,8192]{2,1,0:T(8,128)(2,1)} %param.9) | copy-start | bytes 12582916
  263.6 5.9 %copy-start.1 = (bf16[256,8192]{1,0:T(8,128)(2,1)S(1)}, bf16[256,8192]{1,0:T(8,128)(2,1)}, u32[]{:S(2)}) copy-start(bf16[256,8192]{1,0:T(8,128)(2,1)} %all-reduce.2.cloned.1.call-done) | copy-start | bytes 12582916
  271.8 9.2 %collective-permute-start = (bf16[256,8192]{1,0:T(8,128)(2,1)S(1)}, bf16[256,8192]{1,0:T(8,128)(2,1)}, u32[]{:S(2)}, u32[]{:S(2)}) collective-permute-start(bf16[256,8192]{1,0:T(8,128)(2,1)S(1)} %fusion.10), channel_id=1, source_target_pairs={{32,0},{64,32},{96,64},{33,1},{65,33},{97,65},{34,2},{66,34},{98,6... | collective-permute-start | bytes 12582920 | tf_op jit(solution)/shard_map/ppermute | solution.py:16
Sparse Core Ops, SparseCore 0:
  10.2 54.1 all-gather.4
  66.5 51.2 all-gather.6
  149.6 114.0 all-reduce.1
  267.3 86.0 reduce-scatter.1
where the time goes:
time: 367 us; the launch traced here: 366 us
  waiting for transfers between devices  278 us (76%)
  matrix products  45 us (12%)
  between operations  16 us (4%)
  local copies, waits for them, and re-layouts  13.2 us (4%)
  other arithmetic  12.8 us (3%)
    psum x1, waiting for transfers between devices, on_device(): lax.psum(part.astype(jnp.bfloat16), 'tensor').astype(jnp.float32)  106 us
    reduce_scatter x1, waiting for transfers between devices, on_device(): lax.psum_scatter(lax.dot_general(normed, combined, (((0,), (0,)), ((), ()...  72.4 us
    all_gather x1, waiting for transfers between devices, on_device(): lax.all_gather(value_weight[0], 'dp', axis=0, tiled=True)  45.3 us
    all_gather x1, waiting for transfers between devices, on_device(): lax.all_gather(key_weight[0], 'dp', axis=0, tiled=True)  44.9 us
    dot_general x1, matrix products, on_device(): lax.dot_general(normed, combined, (((0,), (0,)), ((), ())), preferred_ele...  7.92 us
    ppermute x1, waiting for transfers between devices, shifted(): lax.ppermute(value, axis, [(source, source + steps) for source in range(l...  7.89 us
  transfers between devices with their start and end apart: 5, of which 5 were waited for; matrix products, arithmetic and copies ran while one was open for 9% of the time, Pallas kernels for 0%

commit v1 on v0

--- a/solution.py
+++ b/solution.py
@@ -145,7 +145,9 @@
     part = part + lax.dot_general(
         value_grad, value_full, (((1,), (1,)), ((), ())), preferred_element_type=jnp.float32
     )
-    normed_grad = lax.psum(part.astype(jnp.bfloat16), "tensor").astype(jnp.float32)
+    normed_grad = jnp.sum(lax.all_gather(part.astype(jnp.bfloat16), "tensor"), axis=0).astype(
+        jnp.float32
+    )
     section_cot = norm_backward(normed_grad, gain_f, nhat, inv_rms)
     lower = shifted(section_cot, "pipe", -1)
     return (grad_total[:, :kv_cols][None], grad_total[:, kv_cols:][None], lower[None])

time: 367 us -> 359 us (0.978)
  waiting for transfers between devices: 278 us -> 261 us
  other arithmetic: 12.8 us -> 21.2 us
    psum x1 -> x0, waiting for transfers between devices: 106 us -> none  [on_device(): lax.psum(part.astype(jnp.bfloat16), 'tensor').astype(jnp.float32)]
    all_gather x0 -> x1, waiting for transfers between devices: none -> 98.3 us  [on_device(): lax.all_gather(part.astype(jnp.bfloat16), 'tensor')]
    reduce_scatter x1, waiting for transfers between devices: 72.4 us -> 63.3 us  [on_device(): lax.psum_scatter(lax.dot_general(normed, combined, (((0,), (0,)), ((), ()...]
    reduce_sum x0 -> x1, other arithmetic: none -> 8.36 us  [on_device(): jnp.sum(lax.all_gather(part.astype(jnp.bfloat16), 'tensor'), axis=0)]
  transfers between devices with their start and end apart: 5 -> 5, of which waited for: 5 -> 5; matrix products, arithmetic and copies ran while one was open for 9% -> 11% of each run, Pallas kernels for 0% -> 0%
where the time goes in v1:
time: 359 us; the launch traced here: 358 us
  waiting for transfers between devices  261 us (73%)
  matrix products  45 us (13%)
  other arithmetic  21.2 us (6%)
  between operations  16 us (4%)
  local copies, waits for them, and re-layouts  13.5 us (4%)
    all_gather x1, waiting for transfers between devices, on_device(): lax.all_gather(part.astype(jnp.bfloat16), 'tensor')  98.3 us
    reduce_scatter x1, waiting for transfers between devices, on_device(): lax.psum_scatter(lax.dot_general(normed, combined, (((0,), (0,)), ((), ()...  63.3 us
    all_gather x1, waiting for transfers between devices, on_device(): lax.all_gather(value_weight[0], 'dp', axis=0, tiled=True)  45.3 us
    all_gather x1, waiting for transfers between devices, on_device(): lax.all_gather(key_weight[0], 'dp', axis=0, tiled=True)  44.9 us
    reduce_sum x1, other arithmetic, on_device(): jnp.sum(lax.all_gather(part.astype(jnp.bfloat16), 'tensor'), axis=0)  8.36 us
    dot_general x1, matrix products, on_device(): lax.dot_general(normed, combined, (((0,), (0,)), ((), ())), preferred_ele...  7.92 us
    ppermute x1, waiting for transfers between devices, shifted(): lax.ppermute(value, axis, [(source, source + steps) for source in range(l...  7.89 us
    dot_general x1, matrix products, sequence_grads(): jnp.einsum('kgij,ikgd->jkd', score_grad, query_g, preferred_element_type=...  7.24 us
  transfers between devices with their start and end apart: 5, of which 5 were waited for; matrix products, arithmetic and copies ran while one was open for 11% of the time, Pallas kernels for 0%

profile of v1, /device:TPU:0, one launch (start us, length us, event | category | flops | bytes accessed | tf_op | source)
XLA Modules:
  0.0 358.1 jit_solution(18377689535517699296)
XLA Ops:
  7.2 0.0 copy-start.3
  7.2 0.0 all-gather.7.cloned.1.call-start
  7.2 0.7 all-gather.7.cloned.1.call-update
  7.9 0.0 all-gather.9.cloned.1.call-start
  8.0 0.7 all-gather.9.cloned.1.call-update
  8.7 0.0 all-gather.11.cloned.1.call-start
  10.7 0.8 mul.201
  11.5 0.3 multiply_cosine_fusion
  11.9 0.8 copy.12
  12.6 0.8 copy.16
  13.4 2.3 copy.36
  15.7 0.0 copy-done.3
  15.7 0.5 copy.33
  16.2 3.1 fusion.11
  19.3 0.1 fusion.49
  19.4 44.9 %all-gather.7.cloned.1.call-done = bf16[1,8192,256]{2,1,0:T(8,128)(2,1)} async-done(((bf16[1,512,256]{2,1,0:T(8,128)(2,1)}), bf16[1,8192,256]{2,1,0:T(8,128)(2,1)}) %all-gather.7.cloned.1.call-update) | async-done | bytes 4194320 | tf_op jit(solution)/shard_map/all_gather | solution.py:87
  64.3 5.5 %fusion.20 = f32[256,256]{0,1:T(8,128)S(1)} fusion(bf16[1,8192,256]{2,1,0:T(8,128)(2,1)} %all-gather.7.cloned.1.call-done, bf16[1,256,8192]{2,1,0:T(8,128)(2,1)} %param.9, f32[8192]{0:T(1024)S(1)} %bitcast.112, f32[256]{0:T(256)S(1)} %add_rsqrt_fusion), kind=kOutput, calls=%fused_computation.28 | convolution fusion | flops 1082130432 | bytes 8684544 | tf_op jit(solution)/shard_map/dot_general | solution.py:102
  69.9 0.8 copy.13
  70.7 0.1 copy.34
  70.9 0.8 copy.35
  71.7 0.7 negate_bitcast_fusion
  72.4 45.3 %all-gather.9.cloned.1.call-done = bf16[1,8192,256]{2,1,0:T(8,128)(2,1)} async-done(((bf16[1,512,256]{2,1,0:T(8,128)(2,1)}), bf16[1,8192,256]{2,1,0:T(8,128)(2,1)}) %all-gather.9.cloned.1.call-update) | async-done | bytes 4194320 | tf_op jit(solution)/shard_map/all_gather | solution.py:88
  117.7 5.6 %fusion.37 = bf16[256,256]{0,1:T(8,128)(2,1)S(1)} fusion(bf16[1,8192,256]{2,1,0:T(8,128)(2,1)} %all-gather.9.cloned.1.call-done, bf16[1,256,8192]{2,1,0:T(8,128)(2,1)} %param.9, f32[8192]{0:T(1024)S(1)} %bitcast.113, f32[256]{0:T(256)S(1)} %add_rsqrt_fusion), kind=kOutput, calls=%fused_computation.44 | convolution fusion | flops 1082195968 | bytes 8553472 | tf_op jit(solution)/shard_map/dot_general | solution.py:103
  123.3 0.0 copy-start.4
  123.3 2.7 fusion.40
  126.0 0.0 copy-done.4
  126.0 5.0 %fusion.61 = (f32[2,8,256]{2,1,0:T(8,128)S(1)}, f32[2,8,256,256]{2,3,1,0:T(8,128)}) fusion(pred[256,256]{0,1:T(8,128)(4,1)S(1)} %fusion.49, bf16[256,2,8,128]{0,3,2,1:T(8,128)(2,1)S(1)} %bitcast.106, f32[256,2,64]{2,0,1:T(8,128)} %bitcast.117, f32[256,2,64]{2,0,1:T(8,128)} %negate_bitcast_fusion, f32[256,2,128]{2,0,1:T(8,128)} %copy.13, ...), kind=kOutput, calls=%fused_computation.80 | convolution fusion | flops 274006272 | bytes 6111232 | tf_op jit(solution)/shard_map/while/body/eval_jaxpr/sub | solution.py:53
  131.1 3.7 %fusion.34 = bf16[2,128,256]{2,1,0:T(8,128)(2,1)} fusion(f32[256,2,8,128]{0,3,2,1:T(8,128)S(1)} %bitcast.105, f32[256]{0:T(256)S(1)} %broadcast_select_fusion, f32[2,8,256,256]{2,3,1,0:T(8,128)} %get-tuple-element.42, f32[2,8,256]{2,1,0:T(8,128)S(1)} %get-tuple-element.41), kind=kOutput, calls=%fused_computation.43 | convolution fusion | flops 271646720 | bytes 6439936 | tf_op jit(solution)/shard_map/while/body/eval_jaxpr/kgij,ikgd->jkd/dot_general | solution.py:56
  134.7 7.2 %fusion.30 = f32[2,256,128]{1,2,0:T(8,128)S(1)} fusion(bf16[256,2,8,128]{0,3,2,1:T(8,128)(2,1)S(1)} %bitcast.107, f32[2,256,256,8]{2,1,3,0:T(8,128)} %fusion.40, f32[2,8,256,256]{2,3,1,0:T(8,128)} %get-tuple-element.42, f32[2,8,256]{2,1,0:T(8,128)S(1)} %get-tuple-element.41), kind=kOutput, calls=%fused_computation.41 | convolution fusion | flops 275779840 | bytes 9715712 | tf_op jit(solution)/shard_map/while/body/eval_jaxpr/kgij,ikgd->jkd/dot_general | solution.py:62
  142.1 0.0 copy-start.2
  142.1 0.0 copy-start.5
  142.1 3.6 %fusion.18 = f32[256,8192]{1,0:T(8,128)S(1)} fusion(bf16[256,256]{0,1:T(8,128)(2,1)S(1)} %bitcast.110, bf16[1,8192,256]{2,1,0:T(8,128)(2,1)} %all-gather.7.cloned.1.call-done), kind=kOutput, calls=%fused_computation.26 | convolution fusion | flops 1073741824 | bytes 12713984 | tf_op jit(solution)/shard_map/dot_general | solution.py:142
  145.8 0.0 copy-done.2
  145.8 0.0 copy-done.5
  145.8 3.6 %fusion.5 = bf16[256,8192]{1,0:T(8,128)(2,1)} fusion(f32[256,8192]{1,0:T(8,128)S(1)} %fusion.18, bf16[256,256]{0,1:T(8,128)(2,1)S(1)} %bitcast.118, bf16[1,8192,256]{2,1,0:T(8,128)(2,1)S(1)} %copy-done.2), kind=kOutput, calls=%fused_computation.9 | convolution fusion | flops 1077936128 | bytes 16908288 | tf_op jit(solution)/shard_map/dot_general | solution.py:145
  149.4 0.0 all-gather.11.cloned.1.call-update
  149.5 0.0 reduce-scatter.2.cloned.1.call-start
  149.5 7.9 %convolution_convert_fusion = bf16[8192,512]{1,0:T(8,128)(2,1)} fusion(bf16[256,256]{0,1:T(8,128)(2,1)S(1)} %bitcast.119, bf16[256,256]{0,1:T(8,128)(2,1)S(1)} %bitcast.111, bf16[1,256,8192]{2,1,0:T(8,128)(2,1)} %param.9, f32[8192]{0:T(1024)S(1)} %bitcast.114, f32[256]{0:T(256)S(1)} %add_rsqrt_fusion), kind=kOutput, calls=%fused_computation.2 | convolution fusion | flops 2160590848 | bytes 12878848 | tf_op jit(solution)/shard_map/dot_general | solution.py:135
  157.4 0.0 reduce-scatter.2.cloned.1.call-update
  157.5 98.3 %all-gather.11.cloned.1.call-done = bf16[512,8192]{1,0:T(8,128)(2,1)} async-done(((bf16[256,8192]{1,0:T(8,128)(2,1)}), bf16[512,8192]{1,0:T(8,128)(2,1)}) %all-gather.11.cloned.1.call-update) | async-done | bytes 8388624 | tf_op jit(solution)/shard_map/all_gather | solution.py:148
  255.7 8.4 %reduce_sum.53 = bf16[256,8192]{1,0:T(8,128)(2,1)} reduce(bf16[2,256,8192]{2,1,0:T(8,128)(2,1)} %bitcast.103, bf16[]{:T(256)} %constant.53.clone.1), dimensions={0}, to_apply=%region_5.6 | reduce | flops 2097152 | bytes 12582914 | tf_op jit(solution)/shard_map/reduce_sum | solution.py:148
  264.1 0.0 copy-start
  264.1 0.0 copy-start.1
  264.1 5.4 %fusion.7 = f32[256]{0:T(256)S(1)} fusion(bf16[256,8192]{1,0:T(8,128)(2,1)} %reduce_sum.53, bf16[1,256,8192]{2,1,0:T(8,128)(2,1)} %param.9, f32[8192]{0:T(1024)S(1)} %bitcast.115, f32[256]{0:T(256)S(1)} %add_rsqrt_fusion), kind=kLoop, calls=%fused_computation.11 | loop fusion | flops 12582656 | bytes 8423424 | tf_op jit(solution)/shard_map/reduce_sum | solution.py:71
  269.5 0.0 copy-done
  269.5 0.9 copy-done.1
  270.4 2.3 fusion.10
  272.6 1.3 collective-permute-start
  273.9 7.9 %collective-permute-done = bf16[256,8192]{1,0:T(8,128)(2,1)} collective-permute-done((bf16[256,8192]{1,0:T(8,128)(2,1)S(1)}, bf16[256,8192]{1,0:T(8,128)(2,1)}, u32[]{:S(2)}, u32[]{:S(2)}) %collective-permute-start) | collective-permute-done | bytes 4194336 | tf_op jit(solution)/shard_map/ppermute | solution.py:16
  281.8 63.3 %reduce-scatter.2.cloned.1.call-done = bf16[512,512]{1,0:T(8,128)(2,1)} async-done(((bf16[8192,512]{1,0:T(8,128)(2,1)}), bf16[512,512]{1,0:T(8,128)(2,1)}) %reduce-scatter.2.cloned.1.call-update) | async-done | bytes 524304 | tf_op jit(solution)/shard_map/reduce_scatter | solution.py:134
  345.1 1.9 slice_bitcast_fusion
  347.0 4.6 %copy.41 = bf16[1,256,8192]{2,1,0:T(8,128)(2,1)} copy(bf16[1,256,8192]{2,1,0:T(8,128)(2,1)} %bitcast.31) | data formatting | bytes 8388608
  (11 shorter events, 0.2 us)
Async XLA Ops:
  7.2 8.5 %copy-start.3 = (bf16[1,256,2048]{2,1,0:T(8,128)(2,1)S(1)}, bf16[1,256,2048]{2,1,0:T(8,128)(2,1)}, u32[]{:S(2)}) copy-start(bf16[1,256,2048]{2,1,0:T(8,128)(2,1)} %param.14) | copy-start | bytes 3145732
  7.2 57.1 %all-gather.7.cloned.1.call-start = ((), (), s32[]{:S(2)}) async-start(), calls=%async_computation.2 | async-start | bytes 4456448 | tf_op jit(solution)/shard_map/all_gather | solution.py:87
  7.9 109.8 %all-gather.9.cloned.1.call-start = ((), (), s32[]{:S(2)}) async-start(), calls=%async_computation.3 | async-start | bytes 4456448 | tf_op jit(solution)/shard_map/all_gather | solution.py:88
  8.7 247.1 %all-gather.11.cloned.1.call-start = ((), (), s32[]{:S(2)}) async-start(), calls=%async_computation.4 | async-start | bytes 12582912 | tf_op jit(solution)/shard_map/all_gather | solution.py:148
  123.3 2.7 copy-start.4
  142.1 3.7 %copy-start.2 = (bf16[1,8192,256]{2,1,0:T(8,128)(2,1)S(1)}, bf16[1,8192,256]{2,1,0:T(8,128)(2,1)}, u32[]{:S(2)}) copy-start(bf16[1,8192,256]{2,1,0:T(8,128)(2,1)} %all-gather.9.cloned.1.call-done) | copy-start | bytes 12582916
  142.1 3.7 %copy-start.5 = (bf16[2,128,256]{2,1,0:T(8,128)(2,1)S(1)}, bf16[2,128,256]{2,1,0:T(8,128)(2,1)}, u32[]{:S(2)}) copy-start(bf16[2,128,256]{2,1,0:T(8,128)(2,1)} %fusion.34) | copy-start | bytes 393220
  149.5 195.7 %reduce-scatter.2.cloned.1.call-start = ((), (), s32[]{:S(2)}) async-start(), calls=%async_computation.1 | async-start | bytes 8912896 | tf_op jit(solution)/shard_map/reduce_scatter | solution.py:134
  264.1 5.4 %copy-start = (bf16[1,256,8192]{2,1,0:T(8,128)(2,1)S(1)}, bf16[1,256,8192]{2,1,0:T(8,128)(2,1)}, u32[]{:S(2)}) copy-start(bf16[1,256,8192]{2,1,0:T(8,128)(2,1)} %param.9) | copy-start | bytes 12582916
  264.1 6.3 %copy-start.1 = (bf16[256,8192]{1,0:T(8,128)(2,1)S(1)}, bf16[256,8192]{1,0:T(8,128)(2,1)}, u32[]{:S(2)}) copy-start(bf16[256,8192]{1,0:T(8,128)(2,1)} %reduce_sum.53) | copy-start | bytes 12582916
  272.6 9.2 %collective-permute-start = (bf16[256,8192]{1,0:T(8,128)(2,1)S(1)}, bf16[256,8192]{1,0:T(8,128)(2,1)}, u32[]{:S(2)}, u32[]{:S(2)}) collective-permute-start(bf16[256,8192]{1,0:T(8,128)(2,1)S(1)} %fusion.10), channel_id=1, source_target_pairs={{32,0},{64,32},{96,64},{33,1},{65,33},{97,65},{34,2},{66,34},{98,6... | collective-permute-start | bytes 12582920 | tf_op jit(solution)/shard_map/ppermute | solution.py:16
Sparse Core Ops, SparseCore 0:
  10.2 54.1 all-gather.6
  66.5 51.2 all-gather.8
  149.6 106.0 all-gather.10
  259.0 86.1 reduce-scatter.1
